TPU v7x, 128 devices: a whole 4x4x4 slice. The times are simulated.
128 devices in a mesh: row: 8 (over x, core), col: 16 (over y, z).
Axes of the slice: x: 4, y: 4, z: 4, core: 2. Of those that a mesh axis runs over, the one named last changes fastest.
Arguments:
- kernel: float32 [16384, 16384], P('row', 'col'), as said below
Outputs:
- schur: float32 [16384, 16384], P('row', 'col')
- panels: float32 [16384, 768], P('row')
Inputs may be any that keep to these rules, and one draw needn't show every extreme that they name: kernel is symmetric and positive definite with smallest eigenvalue of order one.
All inputs are finite; a program needn't handle non-finite values.
Results may differ from a plain program's by a relative error of at most 0.00027.
Values sent between devices are 32-bit elements; how exact they have to be, the bound alone decides.
No kernel may reach another device: no remote copies, remote signals or barrier semaphores. Data moves between devices by JAX's collectives and lax.ppermute only.
A program may use at most 128 MiB of HBM per device.

v0:
```python
import jax
import jax.numpy as jnp
from jax import lax
from jax.sharding import PartitionSpec as P

BLOCK = 256
STEPS = 3


def spread(array, axis, root):
    mine = lax.axis_index(axis) == root
    return lax.psum(jnp.where(mine, array, jnp.zeros_like(array)), axis)


def place(factor, column, block_ids, step):
    solved = jax.scipy.linalg.solve_triangular(factor, column.T, lower=True).T
    tiled = jnp.tile(factor, (column.shape[0] // factor.shape[0], 1))
    inner = jnp.where((block_ids == step)[:, None], tiled, jnp.float32(0.0))
    return jnp.where((block_ids > step)[:, None], solved, inner)


def pick(panel, col_index, row_count, col_blocks):
    width = panel.shape[1]
    groups = panel.shape[0] // width // col_blocks
    grouped = panel.reshape(col_blocks, groups, width, width)
    chosen = lax.dynamic_index_in_dim(grouped, col_index // row_count, 1, keepdims=False)
    return chosen.reshape(col_blocks * width, width)


def shards(kernel):
    row_count = lax.axis_size("row")
    col_count = lax.axis_size("col")
    row_index = lax.axis_index("row")
    col_index = lax.axis_index("col")
    rows_local, cols_local = kernel.shape
    col_blocks = cols_local // BLOCK
    row_ids = jnp.arange(rows_local) // BLOCK * row_count + row_index
    col_ids = jnp.arange(cols_local) // BLOCK * col_count + col_index
    matrix = kernel
    collected = []
    for step in range(STEPS):
        row_root = step % row_count
        row_slot = step // row_count
        col_root = step % col_count
        col_slot = step // col_count
        corner = matrix[
            row_slot * BLOCK : (row_slot + 1) * BLOCK, col_slot * BLOCK : (col_slot + 1) * BLOCK
        ]
        factor = jnp.linalg.cholesky(corner)
        column = matrix[:, col_slot * BLOCK : (col_slot + 1) * BLOCK]
        factor = spread(factor, "row", row_root)
        panel = spread(place(factor, column, row_ids, step), "col", col_root)
        across = spread(pick(panel, col_index, row_count, col_blocks), "row", col_index % row_count)
        collected.append(panel)
        update = lax.dot_general(
            panel,
            across,
            (((1,), (1,)), ((), ())),
            precision=lax.Precision.HIGHEST,
            preferred_element_type=jnp.float32,
        )
        matrix = matrix - update
    keep = (row_ids >= STEPS)[:, None] & (col_ids >= STEPS)[None, :]
    schur = jnp.where(keep, matrix, jnp.float32(0.0))
    return (schur, jnp.concatenate(collected, axis=1))


def solution(mesh):
    return jax.shard_map(
        shards,
        mesh=mesh,
        in_specs=(P("row", "col"),),
        out_specs=(P("row", "col"), P("row", None)),
        check_vma=False,
    )
```

profile of v0, /device:TPU:0, one launch (start us, length us, event | category | flops | bytes accessed | tf_op | source)
XLA Modules:
  0.0 952.9 jit_solution(7918419507945209357)
XLA Ops:
  18.5 11.7 %cholesky.172 = f32[128,128]{1,0:T(8,128)S(1)} custom-call(f32[128,128]{1,0:T(8,128)S(1)} %cholesky.270), custom_call_target="Cholesky" | custom-call | tf_op jit(solution)/shard_map/jit(cholesky)/cholesky | solution.py:49
  30.2 9.8 %custom-call.15 = f32[1,128,128]{1,2,0:T(8,128)S(1)} custom-call(f32[1,128,128]{2,1,0:T(8,128)S(1)} %get-tuple-element.70), custom_call_target="InvertDiagBlocksLowerTriangular" | custom-call | tf_op jit(solution)/shard_map/jit(cholesky)/cholesky | solution.py:49
  40.5 11.7 %cholesky.189 = f32[128,128]{1,0:T(8,128)S(1)} custom-call(f32[128,128]{1,0:T(8,128)S(1)} %convolution_subtract_fusion.7), custom_call_target="Cholesky" | custom-call | tf_op jit(solution)/shard_map/jit(cholesky)/cholesky | solution.py:49
  57.1 60.3 %all-reduce.11.cloned.1.call-done = f32[256,256]{1,0:T(8,128)} async-done(((f32[256,256]{1,0:T(8,128)}), f32[256,256]{1,0:T(8,128)}) %all-reduce.11.cloned.1.call-update) | async-done | bytes 262160 | tf_op jit(solution)/shard_map/psum | solution.py:12
  122.5 19.7 %custom-call.16 = f32[2,128,128]{1,2,0:T(8,128)S(1)} custom-call(f32[2,128,128]{2,1,0:T(8,128)S(1)} %get-tuple-element.24), custom_call_target="InvertDiagBlocksLowerTriangular" | custom-call | tf_op jit(solution)/shard_map/jit(_solve_triangular)/triangular_solve | solution.py:16
  149.6 89.2 %all-reduce.13.cloned.1.call-done = f32[2048,256]{0,1:T(8,128)} async-done(((f32[2048,256]{0,1:T(8,128)}), f32[2048,256]{0,1:T(8,128)}) %all-reduce.13.cloned.1.call-update) | async-done | bytes 2097168 | tf_op jit(solution)/shard_map/psum | solution.py:12
  246.4 61.7 %all-reduce.15.cloned.1.call-done = f32[1024,256]{0,1:T(8,128)} async-done(((f32[1024,256]{0,1:T(8,128)}), f32[1024,256]{0,1:T(8,128)}) %all-reduce.15.cloned.1.call-update) | async-done | bytes 1048592 | tf_op jit(solution)/shard_map/psum | solution.py:12
  308.1 10.6 %convolution_subtract_fusion.1 = f32[2048,1024]{0,1:T(8,128)S(1)} fusion(f32[2048,1024]{0,1:T(8,128)} %copy.6, f32[2048,256]{0,1:T(8,128)S(1)} %copy-done.2, f32[1024,256]{0,1:T(8,128)} %all-reduce.15.cloned.1.call-done), kind=kOutput, calls=%fused_computation.9 | convolution fusion | flops 6444548096 | bytes 19922944 | tf_op jit(solution)/shard_map/dot_general | solution.py:55
  323.3 11.7 %cholesky.206 = f32[128,128]{1,0:T(8,128)S(1)} custom-call(f32[128,128]{1,0:T(8,128)S(1)} %cholesky.273), custom_call_target="Cholesky" | custom-call | tf_op jit(solution)/shard_map/jit(cholesky)/cholesky | solution.py:49
  335.1 9.8 %custom-call.17 = f32[1,128,128]{1,2,0:T(8,128)S(1)} custom-call(f32[1,128,128]{2,1,0:T(8,128)S(1)} %get-tuple-element.66), custom_call_target="InvertDiagBlocksLowerTriangular" | custom-call | tf_op jit(solution)/shard_map/jit(cholesky)/cholesky | solution.py:49
  345.3 11.7 %cholesky.223 = f32[128,128]{1,0:T(8,128)S(1)} custom-call(f32[128,128]{1,0:T(8,128)S(1)} %convolution_subtract_fusion.6), custom_call_target="Cholesky" | custom-call | tf_op jit(solution)/shard_map/jit(cholesky)/cholesky | solution.py:49
  363.7 56.0 %all-reduce.17.cloned.1.call-done = f32[256,256]{1,0:T(8,128)} async-done(((f32[256,256]{1,0:T(8,128)}), f32[256,256]{1,0:T(8,128)}) %all-reduce.17.cloned.1.call-update) | async-done | bytes 262160 | tf_op jit(solution)/shard_map/psum | solution.py:12
  425.2 19.7 %custom-call.18 = f32[2,128,128]{1,2,0:T(8,128)S(1)} custom-call(f32[2,128,128]{2,1,0:T(8,128)S(1)} %get-tuple-element.25), custom_call_target="InvertDiagBlocksLowerTriangular" | custom-call | tf_op jit(solution)/shard_map/jit(_solve_triangular)/triangular_solve | solution.py:16
  454.7 89.7 %all-reduce.19.cloned.1.call-done = f32[2048,256]{0,1:T(8,128)} async-done(((f32[2048,256]{0,1:T(8,128)}), f32[2048,256]{0,1:T(8,128)}) %all-reduce.19.cloned.1.call-update) | async-done | bytes 2097168 | tf_op jit(solution)/shard_map/psum | solution.py:12
  554.5 61.7 %all-reduce.21.cloned.1.call-done = f32[1024,256]{0,1:T(8,128)} async-done(((f32[1024,256]{0,1:T(8,128)}), f32[1024,256]{0,1:T(8,128)}) %all-reduce.21.cloned.1.call-update) | async-done | bytes 1048592 | tf_op jit(solution)/shard_map/psum | solution.py:12
  616.3 10.7 %convolution_subtract_fusion = f32[2048,1024]{0,1:T(8,128)S(1)} fusion(f32[2048,1024]{0,1:T(8,128)} %copy-done, f32[2048,256]{0,1:T(8,128)} %all-reduce.19.cloned.1.call-done, f32[1024,256]{0,1:T(8,128)} %all-reduce.21.cloned.1.call-done), kind=kOutput, calls=%fused_computation.8 | convolution fusion | flops 6444548096 | bytes 19922944 | tf_op jit(solution)/shard_map/dot_general | solution.py:55
  631.5 11.7 %cholesky.240 = f32[128,128]{1,0:T(8,128)S(1)} custom-call(f32[128,128]{1,0:T(8,128)S(1)} %cholesky.276), custom_call_target="Cholesky" | custom-call | tf_op jit(solution)/shard_map/jit(cholesky)/cholesky | solution.py:49
  643.3 9.8 %custom-call.19 = f32[1,128,128]{1,2,0:T(8,128)S(1)} custom-call(f32[1,128,128]{2,1,0:T(8,128)S(1)} %get-tuple-element.62), custom_call_target="InvertDiagBlocksLowerTriangular" | custom-call | tf_op jit(solution)/shard_map/jit(cholesky)/cholesky | solution.py:49
  653.6 11.7 %cholesky.257 = f32[128,128]{1,0:T(8,128)S(1)} custom-call(f32[128,128]{1,0:T(8,128)S(1)} %convolution_subtract_fusion.5), custom_call_target="Cholesky" | custom-call | tf_op jit(solution)/shard_map/jit(cholesky)/cholesky | solution.py:49
  671.9 56.0 %all-reduce.23.cloned.1.call-done = f32[256,256]{1,0:T(8,128)} async-done(((f32[256,256]{1,0:T(8,128)}), f32[256,256]{1,0:T(8,128)}) %all-reduce.23.cloned.1.call-update) | async-done | bytes 262160 | tf_op jit(solution)/shard_map/psum | solution.py:12
  733.1 19.7 %custom-call.20 = f32[2,128,128]{1,2,0:T(8,128)S(1)} custom-call(f32[2,128,128]{2,1,0:T(8,128)S(1)} %get-tuple-element.26), custom_call_target="InvertDiagBlocksLowerTriangular" | custom-call | tf_op jit(solution)/shard_map/jit(_solve_triangular)/triangular_solve | solution.py:16
  762.6 89.6 %all-reduce.25.cloned.1.call-done = f32[2048,256]{0,1:T(8,128)} async-done(((f32[2048,256]{0,1:T(8,128)}), f32[2048,256]{0,1:T(8,128)}) %all-reduce.25.cloned.1.call-update) | async-done | bytes 2097168 | tf_op jit(solution)/shard_map/psum | solution.py:12
  875.0 49.4 %all-reduce.27.cloned.1.call-done = f32[1024,256]{0,1:T(8,128)} async-done(((f32[1024,256]{0,1:T(8,128)}), f32[1024,256]{0,1:T(8,128)}) %all-reduce.27.cloned.1.call-update) | async-done | bytes 1048592 | tf_op jit(solution)/shard_map/psum | solution.py:12
  924.4 12.3 %subtract_select_fusion = f32[2048,1024]{0,1:T(8,128)} fusion(f32[2048,1024]{0,1:T(8,128)} %copy-done.1, f32[2048,256]{0,1:T(8,128)S(1)} %copy-done.3, f32[1024,256]{0,1:T(8,128)} %all-reduce.27.cloned.1.call-done, pred[2048]{0:T(1024)(128)(4,1)S(1)} %fusion.48, pred[1024]{0:T(1024)(128)(4,1)S(1)} %fusion.52), kind=kOutput, calls=%fused_computation.6 | convolution fusion | flops 6448742400 | bytes 19926016 | tf_op jit(solution)/shard_map/dot_general | solution.py:55
  (142 shorter events, 140.1 us)
Async XLA Ops:
  7.2 110.3 %all-reduce.11.cloned.1.call-start = ((), (), s32[]{:S(2)}) async-start(), calls=%async_computation | async-start | bytes 524288 | tf_op jit(solution)/shard_map/psum | solution.py:12
  55.1 183.6 %all-reduce.13.cloned.1.call-start = ((), (), s32[]{:S(2)}) async-start(), calls=%async_computation.1 | async-start | bytes 4194304 | tf_op jit(solution)/shard_map/psum | solution.py:12
  145.1 1.1 copy-start.8
  149.1 159.0 %all-reduce.15.cloned.1.call-start = ((), (), s32[]{:S(2)}) async-start(), calls=%async_computation.2 | async-start | bytes 2097152 | tf_op jit(solution)/shard_map/psum | solution.py:12
  245.1 63.0 %copy-start.2 = (f32[2048,256]{0,1:T(8,128)S(1)}, f32[2048,256]{0,1:T(8,128)}, u32[]{:S(2)}) copy-start(f32[2048,256]{0,1:T(8,128)} %all-reduce.13.cloned.1.call-done) | copy-start | bytes 6291460
  246.3 173.4 %all-reduce.17.cloned.1.call-start = ((), (), s32[]{:S(2)}) async-start(), calls=%async_computation.3 | async-start | bytes 524288 | tf_op jit(solution)/shard_map/psum | solution.py:12
  318.7 3.4 copy-start
  360.6 183.8 %all-reduce.19.cloned.1.call-start = ((), (), s32[]{:S(2)}) async-start(), calls=%async_computation.4 | async-start | bytes 4194304 | tf_op jit(solution)/shard_map/psum | solution.py:12
  444.9 2.4 copy-start.5
  451.6 1.2 copy-start.6
  454.6 161.6 %all-reduce.21.cloned.1.call-start = ((), (), s32[]{:S(2)}) async-start(), calls=%async_computation.5 | async-start | bytes 2097152 | tf_op jit(solution)/shard_map/psum | solution.py:12
  554.5 173.4 %all-reduce.23.cloned.1.call-start = ((), (), s32[]{:S(2)}) async-start(), calls=%async_computation.6 | async-start | bytes 524288 | tf_op jit(solution)/shard_map/psum | solution.py:12
  627.0 3.4 copy-start.1
  668.7 183.6 %all-reduce.25.cloned.1.call-start = ((), (), s32[]{:S(2)}) async-start(), calls=%async_computation.7 | async-start | bytes 4194304 | tf_op jit(solution)/shard_map/psum | solution.py:12
  752.8 2.4 copy-start.4
  759.5 1.2 copy-start.7
  762.6 161.8 %all-reduce.27.cloned.1.call-start = ((), (), s32[]{:S(2)}) async-start(), calls=%async_computation.8 | async-start | bytes 2097152 | tf_op jit(solution)/shard_map/psum | solution.py:12
  868.3 56.1 %copy-start.3 = (f32[2048,256]{0,1:T(8,128)S(1)}, f32[2048,256]{0,1:T(8,128)}, u32[]{:S(2)}) copy-start(f32[2048,256]{0,1:T(8,128)} %all-reduce.25.cloned.1.call-done) | copy-start | bytes 6291460
Sparse Core Ops, SparseCore 0:
  55.2 62.1 all-reduce.10
  149.2 89.4 all-reduce.12
  246.4 61.6 all-reduce.14
  360.7 59.0 all-reduce.16
  454.7 89.5 all-reduce.18
  554.6 61.6 all-reduce.20
  668.8 59.0 all-reduce.22
  762.7 89.5 all-reduce.24
  862.7 61.6 all-reduce.26
where the time goes:
time: 962 us; the launch traced here: 953 us
  waiting for transfers between devices  614 us (64%)
  other arithmetic  195 us (20%)
  local copies, waits for them, and re-layouts  74.1 us (8%)
  matrix products  49.9 us (5%)
  between operations  18.8 us (2%)
    psum x9, waiting for transfers between devices, spread(): return lax.psum(jnp.where(mine, array, jnp.zeros_like(array)), axis)  614 us
    another operation x20, other arithmetic, shards(): factor = jnp.linalg.cholesky(corner)  103 us
    another operation x7, other arithmetic, place(): solved = jax.scipy.linalg.solve_triangular(factor, column.T, lower=True).T  61.9 us
    unnamed x27, local copies, waits for them, and re-layouts  38.7 us
    dot_general x3, matrix products, shards(): lax.dot_general(panel, across, (((1,), (1,)), ((), ())), precision=lax.Pr...  33.7 us
    select_n x9, other arithmetic, spread(): return lax.psum(jnp.where(mine, array, jnp.zeros_like(array)), axis)  20.7 us
  transfers between devices with their start and end apart: 9, of which 9 were waited for; matrix products, arithmetic and copies ran while one was open for 2% of the time, Pallas kernels for 0%

commit v1 on v0

--- a/solution.py
+++ b/solution.py
@@ -9,7 +9,7 @@
 
 def spread(array, axis, root):
     mine = lax.axis_index(axis) == root
-    return lax.psum(jnp.where(mine, array, jnp.zeros_like(array)), axis)
+    return jnp.sum(lax.all_gather(jnp.where(mine, array, jnp.zeros_like(array)), axis), axis=0)
 
 
 def place(factor, column, block_ids, step):

time: 962 us -> 1270 us (1.32)
  waiting for transfers between devices: 614 us -> 797 us
  local copies, waits for them, and re-layouts: 74.1 us -> 164 us
  other arithmetic: 195 us -> 231 us
    all_gather x0 -> x9, waiting for transfers between devices: none -> 797 us  [spread(): lax.all_gather(jnp.where(mine, array, jnp.zeros_like(array)), axis)]
    psum x9 -> x0, waiting for transfers between devices: 614 us -> none  [spread(): return lax.psum(jnp.where(mine, array, jnp.zeros_like(array)), axis)]
    unnamed x27 -> x23, local copies, waits for them, and re-layouts: 38.7 us -> 124 us
    reduce_sum x0 -> x9, other arithmetic: none -> 44.3 us  [spread(): jnp.sum(lax.all_gather(jnp.where(mine, array, jnp.zeros_like(array)), axi...]
where the time goes in v1:
time: 1270 us; the launch traced here: 1260 us
  waiting for transfers between devices  797 us (63%)
  other arithmetic  231 us (18%)
  local copies, waits for them, and re-layouts  164 us (13%)
  matrix products  48.9 us (4%)
  between operations  18.8 us (1%)
    all_gather x9, waiting for transfers between devices, spread(): lax.all_gather(jnp.where(mine, array, jnp.zeros_like(array)), axis)  797 us
    unnamed x23, local copies, waits for them, and re-layouts  124 us
    another operation x20, other arithmetic, shards(): factor = jnp.linalg.cholesky(corner)  103 us
    another operation x7, other arithmetic, place(): solved = jax.scipy.linalg.solve_triangular(factor, column.T, lower=True).T  59.1 us
    reduce_sum x9, other arithmetic, spread(): jnp.sum(lax.all_gather(jnp.where(mine, array, jnp.zeros_like(array)), axi...  44.3 us
    dot_general x3, matrix products, shards(): lax.dot_general(panel, across, (((1,), (1,)), ((), ())), precision=lax.Pr...  32.2 us
  transfers between devices with their start and end apart: 9, of which 9 were waited for; matrix products, arithmetic and copies ran while one was open for 2% of the time, Pallas kernels for 0%

profile of v1, /device:TPU:0, one launch (start us, length us, event | category | flops | bytes accessed | tf_op | source)
XLA Modules:
  0.0 1261.7 jit_solution(13448989577002801514)
XLA Ops:
  18.5 11.7 cholesky.172
  40.5 11.7 cholesky.189
  58.5 24.4 %all-gather.22.cloned.1.call-done = f32[2048,256]{1,0:T(8,128)} async-done(((f32[256,256]{1,0:T(8,128)}), f32[2048,256]{1,0:T(8,128)}) %all-gather.22.cloned.1.call-update) | async-done | bytes 2097168 | tf_op jit(solution)/shard_map/all_gather | solution.py:12
  89.0 19.7 %custom-call.16 = f32[2,128,128]{1,2,0:T(8,128)S(1)} custom-call(f32[2,128,128]{2,1,0:T(8,128)S(1)} %get-tuple-element.24), custom_call_target="InvertDiagBlocksLowerTriangular" | custom-call | tf_op jit(solution)/shard_map/jit(_solve_triangular)/triangular_solve | solution.py:16
  118.4 197.2 %all-gather.24.cloned.1.call-done = f32[32768,256]{0,1:T(8,128)} async-done(((f32[2048,256]{0,1:T(8,128)}), f32[32768,256]{0,1:T(8,128)}) %all-gather.24.cloned.1.call-update) | async-done | bytes 33554448 | tf_op jit(solution)/shard_map/all_gather | solution.py:12
  315.6 28.8 %copy.35 = f32[32,8,16,2048]{3,2,1,0:T(8,128)S(1)} copy(f32[32,8,16,2048]{3,1,2,0:T(8,128)} %bitcast.162) | data formatting | bytes 67108864
  360.1 49.4 %all-gather.16.cloned.1.call-done = f32[8,1024,256]{2,1,0:T(8,128)} async-done(((f32[1,1024,256]{2,1,0:T(8,128)}), f32[8,1024,256]{2,1,0:T(8,128)}) %all-gather.16.cloned.1.call-update) | async-done | bytes 8388624 | tf_op jit(solution)/shard_map/all_gather | solution.py:12
  413.6 10.1 convolution_subtract_fusion.1
  428.2 11.7 cholesky.206
  450.3 11.7 cholesky.223
  468.7 22.3 %all-gather.26.cloned.1.call-done = f32[2048,256]{1,0:T(8,128)} async-done(((f32[256,256]{1,0:T(8,128)}), f32[2048,256]{1,0:T(8,128)}) %all-gather.26.cloned.1.call-update) | async-done | bytes 2097168 | tf_op jit(solution)/shard_map/all_gather | solution.py:12
  499.6 19.7 %custom-call.18 = f32[2,128,128]{1,2,0:T(8,128)S(1)} custom-call(f32[2,128,128]{2,1,0:T(8,128)S(1)} %get-tuple-element.25), custom_call_target="InvertDiagBlocksLowerTriangular" | custom-call | tf_op jit(solution)/shard_map/jit(_solve_triangular)/triangular_solve | solution.py:16
  525.6 197.6 %all-gather.28.cloned.1.call-done = f32[32768,256]{0,1:T(8,128)} async-done(((f32[2048,256]{0,1:T(8,128)}), f32[32768,256]{0,1:T(8,128)}) %all-gather.28.cloned.1.call-update) | async-done | bytes 33554448 | tf_op jit(solution)/shard_map/all_gather | solution.py:12
  723.2 28.8 %copy.37 = f32[32,8,16,2048]{3,2,1,0:T(8,128)S(1)} copy(f32[32,8,16,2048]{3,1,2,0:T(8,128)} %bitcast.163) | data formatting | bytes 67108864
  770.3 49.4 %all-gather.18.cloned.1.call-done = f32[8,1024,256]{2,1,0:T(8,128)} async-done(((f32[1,1024,256]{2,1,0:T(8,128)}), f32[8,1024,256]{2,1,0:T(8,128)}) %all-gather.18.cloned.1.call-update) | async-done | bytes 8388624 | tf_op jit(solution)/shard_map/all_gather | solution.py:12
  823.7 10.4 convolution_subtract_fusion
  838.7 11.7 cholesky.240
  860.8 11.7 cholesky.257
  879.1 22.2 %all-gather.30.cloned.1.call-done = f32[2048,256]{1,0:T(8,128)} async-done(((f32[256,256]{1,0:T(8,128)}), f32[2048,256]{1,0:T(8,128)}) %all-gather.30.cloned.1.call-update) | async-done | bytes 2097168 | tf_op jit(solution)/shard_map/all_gather | solution.py:12
  909.7 19.7 %custom-call.20 = f32[2,128,128]{1,2,0:T(8,128)S(1)} custom-call(f32[2,128,128]{2,1,0:T(8,128)S(1)} %get-tuple-element.26), custom_call_target="InvertDiagBlocksLowerTriangular" | custom-call | tf_op jit(solution)/shard_map/jit(_solve_triangular)/triangular_solve | solution.py:16
  935.7 197.6 %all-gather.32.cloned.1.call-done = f32[32768,256]{0,1:T(8,128)} async-done(((f32[2048,256]{0,1:T(8,128)}), f32[32768,256]{0,1:T(8,128)}) %all-gather.32.cloned.1.call-update) | async-done | bytes 33554448 | tf_op jit(solution)/shard_map/all_gather | solution.py:12
  1133.3 28.8 %copy.39 = f32[32,8,16,2048]{3,2,1,0:T(8,128)S(1)} copy(f32[32,8,16,2048]{3,1,2,0:T(8,128)} %bitcast.164) | data formatting | bytes 67108864
  1192.9 36.9 %all-gather.20.cloned.1.call-done = f32[8,1024,256]{2,1,0:T(8,128)} async-done(((f32[1,1024,256]{2,1,0:T(8,128)}), f32[8,1024,256]{2,1,0:T(8,128)}) %all-gather.20.cloned.1.call-update) | async-done | bytes 8388624 | tf_op jit(solution)/shard_map/all_gather | solution.py:12
  1233.8 11.7 subtract_select_fusion
  (150 shorter events, 209.8 us)
Async XLA Ops:
  7.2 75.7 %all-gather.22.cloned.1.call-start = ((), (), s32[]{:S(2)}) async-start(), calls=%async_computation.3 | async-start | bytes 2359296 | tf_op jit(solution)/shard_map/all_gather | solution.py:12
  55.1 260.4 %all-gather.24.cloned.1.call-start = ((), (), s32[]{:S(2)}) async-start(), calls=%async_computation.4 | async-start | bytes 35651584 | tf_op jit(solution)/shard_map/all_gather | solution.py:12
  117.9 291.6 %all-gather.16.cloned.1.call-start = ((), (), s32[]{:S(2)}) async-start(), calls=%async_computation | async-start | bytes 9437184 | tf_op jit(solution)/shard_map/all_gather | solution.py:12
  360.1 130.9 %all-gather.26.cloned.1.call-start = ((), (), s32[]{:S(2)}) async-start(), calls=%async_computation.5 | async-start | bytes 2359296 | tf_op jit(solution)/shard_map/all_gather | solution.py:12
  423.7 3.4 copy-start
  465.5 257.7 %all-gather.28.cloned.1.call-start = ((), (), s32[]{:S(2)}) async-start(), calls=%async_computation.6 | async-start | bytes 35651584 | tf_op jit(solution)/shard_map/all_gather | solution.py:12
  519.3 2.4 copy-start.4
  521.7 2.1 copy-start.6
  525.5 294.2 %all-gather.18.cloned.1.call-start = ((), (), s32[]{:S(2)}) async-start(), calls=%async_computation.1 | async-start | bytes 9437184 | tf_op jit(solution)/shard_map/all_gather | solution.py:12
  770.2 131.1 %all-gather.30.cloned.1.call-start = ((), (), s32[]{:S(2)}) async-start(), calls=%async_computation.7 | async-start | bytes 2359296 | tf_op jit(solution)/shard_map/all_gather | solution.py:12
  834.2 3.4 copy-start.1
  875.9 257.4 %all-gather.32.cloned.1.call-start = ((), (), s32[]{:S(2)}) async-start(), calls=%async_computation.8 | async-start | bytes 35651584 | tf_op jit(solution)/shard_map/all_gather | solution.py:12
  929.4 2.4 copy-start.3
  931.8 2.1 copy-start.5
  935.6 294.1 %all-gather.20.cloned.1.call-start = ((), (), s32[]{:S(2)}) async-start(), calls=%async_computation.2 | async-start | bytes 9437184 | tf_op jit(solution)/shard_map/all_gather | solution.py:12
  1192.9 41.0 %copy-start.2 = (f32[2048,256]{0,1:T(8,128)S(1)}, f32[2048,256]{0,1:T(8,128)}, u32[]{:S(2)}) copy-start(f32[2048,256]{0,1:T(8,128)} %bitcast_reduce_fusion) | copy-start | bytes 6291460
Sparse Core Ops, SparseCore 0:
  55.3 27.5 all-gather.21
  118.0 197.5 all-gather.23
  360.2 49.2 all-gather.15
  465.7 25.3 all-gather.25
  525.6 197.5 all-gather.27
  770.4 49.2 all-gather.17
  876.0 25.3 all-gather.29
  935.8 197.5 all-gather.31
  1180.4 49.2 all-gather.19
